TPU v7x, 32 devices: a whole 2x2x4 slice. The times are simulated.
32 devices in a mesh: basis: 2 (over x), eig: 8 (over z, y), chan: 2 (over core).
Axes of the slice: x: 2, y: 2, z: 4, core: 2. Of those that a mesh axis runs over, the one named last changes fastest.
Arguments:
- eigvecs: bfloat16 [512, 5120], P('eig', 'basis'), may hold values from -6 to 6
- boundary: bfloat16 [5120, 4096], P('basis', 'chan'), may hold values from -0.3125 to 0.3125
- block_sizes: int32 [16], replicated, may hold values from 256 to 768, as said below
- target_of_channel: int32 [4096], P('chan'), may hold values from 0 to 15, as said below
- poles: float32 [512], replicated, may hold values from -4 to 4, as said below
- energies: float32 [16], P('basis'), may hold values from -0.25 to 0.25
Outputs:
- rmatrix: float32 [16, 4096, 4096], P('basis', 'chan', 'eig')
Inputs may be any that keep to these rules, and one draw needn't show every extreme that they name: `poles`: every pole lies 0.5 or more away from zero, with both signs present. `block_sizes`: the sizes sum to 5120; every target state's block holds at least 256 basis rows. `target_of_channel`: every target state has exactly 256 channels.
All inputs are finite; a program needn't handle non-finite values.
Results may differ from a plain program's by a relative error of at most 0.0049.
Values may be sent and summed in bfloat16 or wider, within the bound.
No kernel may reach another device: no remote copies, remote signals or barrier semaphores. Data moves between devices by JAX's collectives and lax.ppermute only.
A program may use at most 128 MiB of HBM per device.

v0:
```python
import jax
import jax.numpy as jnp
from jax import lax
from jax.sharding import PartitionSpec as P


def per_device(eigvecs, boundary, block_sizes, target_of_channel, poles, energies):
    rows_here = eigvecs.shape[1]
    block_ends = jnp.cumsum(block_sizes)
    row_ids = lax.axis_index("basis") * rows_here + jnp.arange(rows_here, dtype=jnp.int32)
    owner_of = jnp.sum((block_ends[None, :] <= row_ids[:, None]).astype(jnp.int32), axis=1)
    member = owner_of[:, None] == target_of_channel[None, :]
    masked = jnp.where(member, boundary, jnp.zeros_like(boundary))
    partial_value = jnp.dot(eigvecs, masked, preferred_element_type=jnp.float32)
    amplitudes = lax.psum(partial_value, "basis").astype(jnp.bfloat16)
    all_channels = lax.all_gather(amplitudes, "chan", axis=1, tiled=True)
    own_width = amplitudes.shape[1]
    own_first = lax.axis_index("chan") * own_width
    col_width = all_channels.shape[1] // lax.axis_size("eig")
    col_first = lax.axis_index("eig") * col_width
    factor = poles.shape[0] ** (-0.5)
    weights = 1.0 / (poles[None, :] - energies[:, None])
    panel_in = lax.all_gather(all_channels, "eig", axis=0, tiled=True)
    left_panel = lax.dynamic_slice_in_dim(panel_in, own_first, own_width, 1)
    right_panel = lax.dynamic_slice_in_dim(panel_in, col_first, col_width, 1)
    scaled = (weights[:, :, None] * left_panel[None].astype(jnp.float32)).astype(jnp.bfloat16)
    summed = jnp.einsum("ekc,kd->ecd", scaled, right_panel, preferred_element_type=jnp.float32)
    return summed * factor


def solution(mesh):
    placed = (P("eig", "basis"), P("basis", "chan"), P(), P("chan"), P(), P("basis"))
    return jax.shard_map(
        per_device, mesh=mesh, in_specs=placed, out_specs=P("basis", "chan", "eig"), check_vma=False
    )
```

profile of v0, /device:TPU:0, one launch (start us, length us, event | category | flops | bytes accessed | tf_op | source)
XLA Modules:
  0.0 140.8 jit_solution(5083630222662826893)
XLA Ops:
  6.5 0.0 copy-start
  6.5 0.0 all-gather.2.cloned.1.call-start
  6.5 0.8 copy.11
  7.4 0.1 reduce
  7.5 0.1 convert_reduce_fusion
  7.6 0.0 copy-done
  7.6 0.0 copy-start.1
  7.6 0.0 copy-start.2
  7.6 6.4 %fusion.6 = f32[64,2048]{1,0:T(8,128)S(1)} fusion(bf16[64,2560]{1,0:T(8,128)(2,1)S(1)} %copy-done, bf16[2560,2048]{1,0:T(8,128)(2,1)} %param.7, s32[2048]{0:T(1024)} %param.9, s32[2560]{0:T(1024)S(1)} %convert_reduce_fusion), kind=kOutput, calls=%fused_computation.9 | convolution fusion | flops 681574400 | bytes 11356160 | tf_op jit(solution)/shard_map/dot_general | solution.py:14
  14.0 18.6 %all-reduce.1 = bf16[64,2048]{1,0:T(8,128)(2,1)S(1)} all-reduce(f32[64,2048]{1,0:T(8,128)S(1)} %fusion.6), channel_id=1, replica_groups=mesh['basis'=2,'eig'=8,'chan'=2] {'basis'}, use_global_device_ids=true, to_apply=%region_2.3 | all-reduce | flops 131072 | bytes 786432 | tf_op jit(solution)/shard_map/psum | solution.py:15
  32.6 2.3 %all_gather.6 = bf16[64,4096]{1,0:T(8,128)(2,1)} all-gather(bf16[64,2048]{1,0:T(8,128)(2,1)S(1)} %all-reduce.1), channel_id=1, replica_groups=mesh['basis'=2,'eig'=8,'chan'=2] {'chan'}, dimensions={1}, use_global_device_ids=true | all-gather | bytes 786432 | tf_op jit(solution)/shard_map/all_gather | solution.py:16
  34.9 0.0 all-gather.2.cloned.1.call-update
  35.0 0.0 copy-done.1
  35.0 0.0 copy-done.2
  35.0 0.1 subtract_divide_fusion
  35.1 73.2 %all-gather.2.cloned.1.call-done = bf16[512,4096]{1,0:T(8,128)(2,1)} async-done(((bf16[64,4096]{1,0:T(8,128)(2,1)}), bf16[512,4096]{1,0:T(8,128)(2,1)}) %all-gather.2.cloned.1.call-update) | async-done | bytes 4194320 | tf_op jit(solution)/shard_map/all_gather | solution.py:23
  108.2 4.1 %dynamic-slice_convert_fusion = f32[512,2048]{1,0:T(8,128)} fusion(bf16[512,4096]{1,0:T(8,128)(2,1)} %all-gather.2.cloned.1.call-done, s32[]{:T(128)S(6)} %select_n.11), kind=kLoop, calls=%fused_computation.10 | loop fusion | flops 1048576 | bytes 6291460 | tf_op jit(solution)/shard_map/convert_element_type | solution.py:26
  112.4 5.3 %copy.12 = f32[512,2048]{0,1:T(8,128)} copy(f32[512,2048]{1,0:T(8,128)} %dynamic-slice_convert_fusion) | data formatting | bytes 8388608 | tf_op jit(solution)/shard_map/convert_element_type | solution.py:26
  117.7 16.3 %convolution_multiply_fusion = f32[8,2048,512]{2,1,0:T(8,128)} fusion(f32[512,2048]{0,1:T(8,128)} %copy.12, f32[8,512]{1,0:T(8,128)S(1)} %subtract_divide_fusion, bf16[512,4096]{1,0:T(8,128)(2,1)} %all-gather.2.cloned.1.call-done, s32[]{:T(128)S(6)} %select_n.12), kind=kOutput, calls=%fused_computation.2 | convolution fusion | flops 8615100416 | bytes 38289412 | tf_op jit(solution)/shard_map/ekc,kd->ecd/dot_general | solution.py:27
  (2 shorter events, 0.0 us)
Async XLA Ops:
  6.5 1.1 copy-start
  6.5 101.7 %all-gather.2.cloned.1.call-start = ((), (), s32[]{:S(2)}) async-start(), calls=%async_computation | async-start | bytes 4718592 | tf_op jit(solution)/shard_map/all_gather | solution.py:23
  7.6 27.4 %copy-start.1 = (f32[512]{0:T(512)S(1)}, f32[512]{0:T(512)}, u32[]{:S(2)}) copy-start(f32[512]{0:T(512)} %param.10) | copy-start | bytes 6148
  7.6 27.4 %copy-start.2 = (f32[8]{0:T(128)S(1)}, f32[8]{0:T(128)}, u32[]{:S(2)}) copy-start(f32[8]{0:T(128)} %param.11) | copy-start | bytes 100
Sparse Core Ops, SparseCore 0:
  35.1 73.1 all-gather.1
where the time goes:
time: 141 us
  waiting for transfers between devices  73.2 us (52%)
  matrix products  22.7 us (16%)
  blocking collectives  20.9 us (15%)
  between operations  13.5 us (10%)
  local copies, waits for them, and re-layouts  6.14 us (4%)
  other arithmetic  4.47 us (3%)
    all_gather x1, waiting for transfers between devices, per_device(): panel_in = lax.all_gather(all_channels, 'eig', axis=0, tiled=True)  73.2 us
    psum x1, blocking collectives, per_device(): amplitudes = lax.psum(partial_value, 'basis').astype(jnp.bfloat16)  18.6 us
    dot_general x1, matrix products, per_device(): jnp.einsum('ekc,kd->ecd', scaled, right_panel, preferred_element_type=jnp...  16.3 us
    dot_general x1, matrix products, per_device(): partial_value = jnp.dot(eigvecs, masked, preferred_element_type=jnp.float32)  6.39 us
    convert_element_type x1, local copies, waits for them, and re-layouts, per_device(): left_panel[None].astype(jnp.float32)  5.34 us
    convert_element_type x1, other arithmetic, per_device(): left_panel[None].astype(jnp.float32)  4.13 us
  transfers between devices with their start and end apart: 1, of which 1 were waited for; matrix products, arithmetic and copies ran while one was open for 0% of the time, Pallas kernels for 0%

commit v1 on v0

--- a/solution.py
+++ b/solution.py
@@ -20,7 +20,26 @@
     col_first = lax.axis_index("eig") * col_width
     factor = poles.shape[0] ** (-0.5)
     weights = 1.0 / (poles[None, :] - energies[:, None])
-    panel_in = lax.all_gather(all_channels, "eig", axis=0, tiled=True)
+    devices, index, extent = (lax.axis_size("eig"), lax.axis_index("eig"), all_channels.shape[0])
+    upward = [(i, (i + 1) % devices) for i in range(devices)]
+    behind = [(i, (i - 1) % devices) for i in range(devices)]
+    panel_in = jnp.zeros(
+        (*all_channels.shape[:0], devices * extent, *all_channels.shape[0 + 1 :]),
+        all_channels.dtype,
+    )
+    panel_in = lax.dynamic_update_slice_in_dim(panel_in, all_channels, index * extent, axis=0)
+    from_left = from_right = all_channels
+    half = devices // 2
+    for step in range(1, half + 1):
+        from_left = lax.ppermute(from_left, "eig", upward)
+        panel_in = lax.dynamic_update_slice_in_dim(
+            panel_in, from_left, (index - step) % devices * extent, axis=0
+        )
+        if step < devices - half:
+            from_right = lax.ppermute(from_right, "eig", behind)
+            panel_in = lax.dynamic_update_slice_in_dim(
+                panel_in, from_right, (index + step) % devices * extent, axis=0
+            )
     left_panel = lax.dynamic_slice_in_dim(panel_in, own_first, own_width, 1)
     right_panel = lax.dynamic_slice_in_dim(panel_in, col_first, col_width, 1)
     scaled = (weights[:, :, None] * left_panel[None].astype(jnp.float32)).astype(jnp.bfloat16)

time: 141 us -> 146 us (1.035)
  between operations: 13.5 us -> 0.23 us
  starting transfers between devices: 0.01 us -> 12.2 us
  waiting for transfers between devices: 73.2 us -> 77.7 us
  local copies, waits for them, and re-layouts: 6.14 us -> 8.93 us
  other arithmetic: 4.47 us -> 2.88 us
    ppermute x0 -> x7, waiting for transfers between devices: none -> 77.7 us  [the longest x3 41.6 us: per_device(): from_right = lax.ppermute(from_right, 'eig', behind)]
    all_gather x1 -> x0, waiting for transfers between devices: 73.2 us -> none  [per_device(): panel_in = lax.all_gather(all_channels, 'eig', axis=0, tiled=True)]
    ppermute x0 -> x7, starting transfers between devices: none -> 12.2 us  [the longest x3 9.72 us: per_device(): from_right = lax.ppermute(from_right, 'eig', behind)]
    unnamed x6 -> x8, local copies, waits for them, and re-layouts: 0.02 us -> 1.98 us
    convert_element_type x1, other arithmetic: 4.13 us -> 2.54 us  [per_device(): left_panel[None].astype(jnp.float32)]
  transfers between devices with their start and end apart: 1 -> 7, of which waited for: 1 -> 4; matrix products, arithmetic and copies ran while one was open for 0% -> 1% of each run, Pallas kernels for 0% -> 0%
where the time goes in v1:
time: 146 us; the launch traced here: 145 us
  waiting for transfers between devices  77.7 us (53%)
  matrix products  22.7 us (16%)
  blocking collectives  20.8 us (14%)
  starting transfers between devices  12.2 us (8%)
  local copies, waits for them, and re-layouts  8.93 us (6%)
  other arithmetic  2.88 us (2%)
    ppermute x3, waiting for transfers between devices, per_device(): from_right = lax.ppermute(from_right, 'eig', behind)  41.6 us
    ppermute x4, waiting for transfers between devices, per_device(): from_left = lax.ppermute(from_left, 'eig', upward)  36.1 us
    psum x1, blocking collectives, per_device(): amplitudes = lax.psum(partial_value, 'basis').astype(jnp.bfloat16)  18.6 us
    dot_general x1, matrix products, per_device(): jnp.einsum('ekc,kd->ecd', scaled, right_panel, preferred_element_type=jnp...  16.3 us
    ppermute x3, starting transfers between devices, per_device(): from_right = lax.ppermute(from_right, 'eig', behind)  9.72 us
    dot_general x1, matrix products, per_device(): partial_value = jnp.dot(eigvecs, masked, preferred_element_type=jnp.float32)  6.39 us
    convert_element_type x1, local copies, waits for them, and re-layouts, per_device(): left_panel[None].astype(jnp.float32)  5.35 us
  transfers between devices with their start and end apart: 7, of which 4 were waited for; matrix products, arithmetic and copies ran while one was open for 1% of the time, Pallas kernels for 0%

profile of v1, /device:TPU:0, one launch (start us, length us, event | category | flops | bytes accessed | tf_op | source)
XLA Modules:
  0.0 145.4 jit_solution(13631930627231229600)
XLA Ops:
  0.0 0.8 copy.11
  0.8 0.1 reduce
  0.9 0.1 convert_reduce_fusion
  1.1 0.0 copy-start.2
  1.1 0.0 copy-start.3
  1.1 6.4 %fusion.6 = f32[64,2048]{1,0:T(8,128)S(1)} fusion(bf16[64,2560]{1,0:T(8,128)(2,1)S(1)} %copy-done, bf16[2560,2048]{1,0:T(8,128)(2,1)} %param.7, s32[2048]{0:T(1024)} %param.9, s32[2560]{0:T(1024)S(1)} %convert_reduce_fusion), kind=kOutput, calls=%fused_computation.9 | convolution fusion | flops 681574400 | bytes 11356160 | tf_op jit(solution)/shard_map/dot_general | solution.py:14
  7.5 18.6 %all-reduce.1 = bf16[64,2048]{1,0:T(8,128)(2,1)S(1)} all-reduce(f32[64,2048]{1,0:T(8,128)S(1)} %fusion.6), channel_id=1, replica_groups=mesh['basis'=2,'eig'=8,'chan'=2] {'basis'}, use_global_device_ids=true, to_apply=%region_2.3 | all-reduce | flops 131072 | bytes 786432 | tf_op jit(solution)/shard_map/psum | solution.py:15
  26.1 2.2 %all_gather.3 = bf16[64,4096]{1,0:T(8,128)(2,1)S(1)} all-gather(bf16[64,2048]{1,0:T(8,128)(2,1)S(1)} %all-reduce.1), channel_id=1, replica_groups=mesh['basis'=2,'eig'=8,'chan'=2] {'chan'}, dimensions={1}, use_global_device_ids=true | all-gather | bytes 786432 | tf_op jit(solution)/shard_map/all_gather | solution.py:16
  28.3 4.6 %collective-permute-start.1 = (bf16[64,4096]{1,0:T(8,128)(2,1)S(1)}, bf16[64,4096]{1,0:T(8,128)(2,1)S(1)}, u32[]{:S(2)}, u32[]{:S(2)}) collective-permute-start(bf16[64,4096]{1,0:T(8,128)(2,1)S(1)} %all_gather.3), channel_id=1, source_target_pairs={{0,14},{2,0},{4,2},{6,4},{8,6},{10,8},{12,10},{14,12},{1,15},{3,1}... | collective-permute-start | bytes 1572872 | tf_op jit(solution)/shard_map/ppermute | solution.py:39
  32.8 0.0 collective-permute-start
  32.8 0.1 subtract_divide_fusion
  33.0 0.5 broadcast_in_dim.4
  33.6 19.9 %collective-permute-done.1 = bf16[64,4096]{1,0:T(8,128)(2,1)S(1)} collective-permute-done((bf16[64,4096]{1,0:T(8,128)(2,1)S(1)}, bf16[64,4096]{1,0:T(8,128)(2,1)S(1)}, u32[]{:S(2)}, u32[]{:S(2)}) %collective-permute-start.1) | collective-permute-done | bytes 524320 | tf_op jit(solution)/shard_map/ppermute | solution.py:39
  53.5 2.6 %collective-permute-start.3 = (bf16[64,4096]{1,0:T(8,128)(2,1)S(1)}, bf16[64,4096]{1,0:T(8,128)(2,1)S(1)}, u32[]{:S(2)}, u32[]{:S(2)}) collective-permute-start(bf16[64,4096]{1,0:T(8,128)(2,1)S(1)} %collective-permute-done.1), channel_id=1, source_target_pairs={{0,14},{2,0},{4,2},{6,4},{8,6},{10,8},{12,10},{14,12},{1,15},{3,1}... | collective-permute-start | bytes 1572872 | tf_op jit(solution)/shard_map/ppermute | solution.py:39
  56.1 0.0 collective-permute-done
  56.2 21.7 %collective-permute-done.3 = bf16[64,4096]{1,0:T(8,128)(2,1)S(1)} collective-permute-done((bf16[64,4096]{1,0:T(8,128)(2,1)S(1)}, bf16[64,4096]{1,0:T(8,128)(2,1)S(1)}, u32[]{:S(2)}, u32[]{:S(2)}) %collective-permute-start.3) | collective-permute-done | bytes 524320 | tf_op jit(solution)/shard_map/ppermute | solution.py:39
  77.8 2.6 %collective-permute-start.5 = (bf16[64,4096]{1,0:T(8,128)(2,1)S(1)}, bf16[64,4096]{1,0:T(8,128)(2,1)S(1)}, u32[]{:S(2)}, u32[]{:S(2)}) collective-permute-start(bf16[64,4096]{1,0:T(8,128)(2,1)S(1)} %collective-permute-done.3), channel_id=1, source_target_pairs={{0,14},{2,0},{4,2},{6,4},{8,6},{10,8},{12,10},{14,12},{1,15},{3,1}... | collective-permute-start | bytes 1572872 | tf_op jit(solution)/shard_map/ppermute | solution.py:39
  80.5 19.9 %collective-permute-done.4 = bf16[64,4096]{1,0:T(8,128)(2,1)S(1)} collective-permute-done((bf16[64,4096]{1,0:T(8,128)(2,1)S(1)}, bf16[64,4096]{1,0:T(8,128)(2,1)S(1)}, u32[]{:S(2)}, u32[]{:S(2)}) %collective-permute-start.4) | collective-permute-done | bytes 524320 | tf_op jit(solution)/shard_map/ppermute | solution.py:34
  100.4 2.5 %collective-permute-start.6 = (bf16[64,4096]{1,0:T(8,128)(2,1)S(1)}, bf16[64,4096]{1,0:T(8,128)(2,1)S(1)}, u32[]{:S(2)}, u32[]{:S(2)}) collective-permute-start(bf16[64,4096]{1,0:T(8,128)(2,1)S(1)} %collective-permute-done.4), channel_id=1, source_target_pairs={{0,2},{2,4},{4,6},{6,8},{8,10},{10,12},{12,14},{14,0},{1,3},{3,5},... | collective-permute-start | bytes 1572872 | tf_op jit(solution)/shard_map/ppermute | solution.py:34
  103.0 16.3 %collective-permute-done.6 = bf16[64,4096]{1,0:T(8,128)(2,1)S(1)} collective-permute-done((bf16[64,4096]{1,0:T(8,128)(2,1)S(1)}, bf16[64,4096]{1,0:T(8,128)(2,1)S(1)}, u32[]{:S(2)}, u32[]{:S(2)}) %collective-permute-start.6) | collective-permute-done | bytes 524320 | tf_op jit(solution)/shard_map/ppermute | solution.py:34
  119.3 2.0 %copy-done.1 = bf16[512,4096]{1,0:T(8,128)(2,1)} copy-done((bf16[512,4096]{1,0:T(8,128)(2,1)}, bf16[512,4096]{1,0:T(8,128)(2,1)S(1)}, u32[]{:S(2)}) %copy-start.1) | copy-done | bytes 4194328
  121.2 2.5 %dynamic-slice_convert_fusion = f32[512,2048]{1,0:T(8,128)} fusion(bf16[512,4096]{1,0:T(8,128)(2,1)S(1)} %constant_dynamic-update-slice_fusion, s32[]{:T(128)S(6)} %select_n.81), kind=kLoop, calls=%fused_computation.10 | loop fusion | flops 1048576 | bytes 6291460 | tf_op jit(solution)/shard_map/convert_element_type | solution.py:45
  123.8 5.3 %copy.12 = f32[512,2048]{0,1:T(8,128)} copy(f32[512,2048]{1,0:T(8,128)} %dynamic-slice_convert_fusion) | data formatting | bytes 8388608 | tf_op jit(solution)/shard_map/convert_element_type | solution.py:45
  129.1 16.3 %convolution_multiply_fusion = f32[8,2048,512]{2,1,0:T(8,128)} fusion(f32[512,2048]{0,1:T(8,128)} %copy.12, f32[8,512]{1,0:T(8,128)S(1)} %subtract_divide_fusion, bf16[512,4096]{1,0:T(8,128)(2,1)} %copy-done.1, s32[]{:T(128)S(6)} %select_n.82), kind=kOutput, calls=%fused_computation.2 | convolution fusion | flops 8615100416 | bytes 38289412 | tf_op jit(solution)/shard_map/ekc,kd->ecd/dot_general | solution.py:46
  (19 shorter events, 0.4 us)
Async XLA Ops:
  0.0 1.1 copy-start
  1.1 31.8 %copy-start.2 = (f32[512]{0:T(512)S(1)}, f32[512]{0:T(512)}, u32[]{:S(2)}) copy-start(f32[512]{0:T(512)} %param.10) | copy-start | bytes 6148
  1.1 31.8 %copy-start.3 = (f32[8]{0:T(128)S(1)}, f32[8]{0:T(128)}, u32[]{:S(2)}) copy-start(f32[8]{0:T(128)} %param.11) | copy-start | bytes 100
  28.3 25.2 %collective-permute-start.1 = (bf16[64,4096]{1,0:T(8,128)(2,1)S(1)}, bf16[64,4096]{1,0:T(8,128)(2,1)S(1)}, u32[]{:S(2)}, u32[]{:S(2)}) collective-permute-start(bf16[64,4096]{1,0:T(8,128)(2,1)S(1)} %all_gather.3), channel_id=1, source_target_pairs={{0,14},{2,0},{4,2},{6,4},{8,6},{10,8},{12,10},{14,12},{1,15},{3,1}... | collective-permute-start | bytes 1572872 | tf_op jit(solution)/shard_map/ppermute | solution.py:39
  32.8 23.2 %collective-permute-start = (bf16[64,4096]{1,0:T(8,128)(2,1)S(1)}, bf16[64,4096]{1,0:T(8,128)(2,1)S(1)}, u32[]{:S(2)}, u32[]{:S(2)}) collective-permute-start(bf16[64,4096]{1,0:T(8,128)(2,1)S(1)} %all_gather.3), channel_id=1, source_target_pairs={{0,2},{2,4},{4,6},{6,8},{8,10},{10,12},{12,14},{14,0},{1,3},{3,5},... | collective-permute-start | bytes 1572872 | tf_op jit(solution)/shard_map/ppermute | solution.py:34
  53.5 24.3 %collective-permute-start.3 = (bf16[64,4096]{1,0:T(8,128)(2,1)S(1)}, bf16[64,4096]{1,0:T(8,128)(2,1)S(1)}, u32[]{:S(2)}, u32[]{:S(2)}) collective-permute-start(bf16[64,4096]{1,0:T(8,128)(2,1)S(1)} %collective-permute-done.1), channel_id=1, source_target_pairs={{0,14},{2,0},{4,2},{6,4},{8,6},{10,8},{12,10},{14,12},{1,15},{3,1}... | collective-permute-start | bytes 1572872 | tf_op jit(solution)/shard_map/ppermute | solution.py:39
  56.1 24.3 %collective-permute-start.2 = (bf16[64,4096]{1,0:T(8,128)(2,1)S(1)}, bf16[64,4096]{1,0:T(8,128)(2,1)S(1)}, u32[]{:S(2)}, u32[]{:S(2)}) collective-permute-start(bf16[64,4096]{1,0:T(8,128)(2,1)S(1)} %collective-permute-done), channel_id=1, source_target_pairs={{0,2},{2,4},{4,6},{6,8},{8,10},{10,12},{12,14},{14,0},{1,3},{3,5},... | collective-permute-start | bytes 1572872 | tf_op jit(solution)/shard_map/ppermute | solution.py:34
  77.8 25.1 %collective-permute-start.5 = (bf16[64,4096]{1,0:T(8,128)(2,1)S(1)}, bf16[64,4096]{1,0:T(8,128)(2,1)S(1)}, u32[]{:S(2)}, u32[]{:S(2)}) collective-permute-start(bf16[64,4096]{1,0:T(8,128)(2,1)S(1)} %collective-permute-done.3), channel_id=1, source_target_pairs={{0,14},{2,0},{4,2},{6,4},{8,6},{10,8},{12,10},{14,12},{1,15},{3,1}... | collective-permute-start | bytes 1572872 | tf_op jit(solution)/shard_map/ppermute | solution.py:39
  80.4 20.0 %collective-permute-start.4 = (bf16[64,4096]{1,0:T(8,128)(2,1)S(1)}, bf16[64,4096]{1,0:T(8,128)(2,1)S(1)}, u32[]{:S(2)}, u32[]{:S(2)}) collective-permute-start(bf16[64,4096]{1,0:T(8,128)(2,1)S(1)} %collective-permute-done.2), channel_id=1, source_target_pairs={{0,2},{2,4},{4,6},{6,8},{8,10},{10,12},{12,14},{14,0},{1,3},{3,5},... | collective-permute-start | bytes 1572872 | tf_op jit(solution)/shard_map/ppermute | solution.py:34
  100.4 18.8 %collective-permute-start.6 = (bf16[64,4096]{1,0:T(8,128)(2,1)S(1)}, bf16[64,4096]{1,0:T(8,128)(2,1)S(1)}, u32[]{:S(2)}, u32[]{:S(2)}) collective-permute-start(bf16[64,4096]{1,0:T(8,128)(2,1)S(1)} %collective-permute-done.4), channel_id=1, source_target_pairs={{0,2},{2,4},{4,6},{6,8},{8,10},{10,12},{12,14},{14,0},{1,3},{3,5},... | collective-permute-start | bytes 1572872 | tf_op jit(solution)/shard_map/ppermute | solution.py:34
  119.3 2.0 %copy-start.1 = (bf16[512,4096]{1,0:T(8,128)(2,1)}, bf16[512,4096]{1,0:T(8,128)(2,1)S(1)}, u32[]{:S(2)}) copy-start(bf16[512,4096]{1,0:T(8,128)(2,1)S(1)} %constant_dynamic-update-slice_fusion) | copy-start | bytes 12582916

commit v2 on v0

--- a/solution.py
+++ b/solution.py
@@ -1,7 +1,16 @@
+import functools
 import jax
 import jax.numpy as jnp
 from jax import lax
 from jax.sharding import PartitionSpec as P
+
+
+def _follow_roots(panel, axis_key):
+    plain = lax.all_gather(panel, axis_key).sum(axis=0)
+    return plain
+
+
+list_steps_all = functools.partial(_follow_roots, axis_key="basis")
 
 
 def per_device(eigvecs, boundary, block_sizes, target_of_channel, poles, energies):
@@ -12,7 +21,7 @@
     member = owner_of[:, None] == target_of_channel[None, :]
     masked = jnp.where(member, boundary, jnp.zeros_like(boundary))
     partial_value = jnp.dot(eigvecs, masked, preferred_element_type=jnp.float32)
-    amplitudes = lax.psum(partial_value, "basis").astype(jnp.bfloat16)
+    amplitudes = list_steps_all(partial_value).astype(jnp.bfloat16)
     all_channels = lax.all_gather(amplitudes, "chan", axis=1, tiled=True)
     own_width = amplitudes.shape[1]
     own_first = lax.axis_index("chan") * own_width

time: 141 us -> 148 us (1.050)
  waiting for transfers between devices: 73.2 us -> 97 us
  blocking collectives: 20.9 us -> 2.31 us
    all_gather x0 -> x1, waiting for transfers between devices: none -> 24.1 us  [_follow_roots(): plain = lax.all_gather(panel, axis_key).sum(axis=0)]
    psum x1 -> x0, blocking collectives: 18.6 us -> none  [per_device(): amplitudes = lax.psum(partial_value, 'basis').astype(jnp.bfloat16)]
  transfers between devices with their start and end apart: 1 -> 2, of which waited for: 1 -> 2; matrix products, arithmetic and copies ran while one was open for 0% -> 0% of each run, Pallas kernels for 0% -> 0%
where the time goes in v2:
time: 148 us
  waiting for transfers between devices  97 us (66%)
  matrix products  23.5 us (16%)
  between operations  13.5 us (9%)
  local copies, waits for them, and re-layouts  6.14 us (4%)
  other arithmetic  5.79 us (4%)
  blocking collectives  2.31 us (2%)
    all_gather x1, waiting for transfers between devices, per_device(): panel_in = lax.all_gather(all_channels, 'eig', axis=0, tiled=True)  72.9 us
    all_gather x1, waiting for transfers between devices, _follow_roots(): plain = lax.all_gather(panel, axis_key).sum(axis=0)  24.1 us
    dot_general x1, matrix products, per_device(): jnp.einsum('ekc,kd->ecd', scaled, right_panel, preferred_element_type=jnp...  16.3 us
    dot_general x1, matrix products, per_device(): partial_value = jnp.dot(eigvecs, masked, preferred_element_type=jnp.float32)  7.18 us
    convert_element_type x1, local copies, waits for them, and re-layouts, per_device(): left_panel[None].astype(jnp.float32)  5.34 us
    convert_element_type x1, other arithmetic, per_device(): left_panel[None].astype(jnp.float32)  4.13 us
  transfers between devices with their start and end apart: 2, of which 2 were waited for; matrix products, arithmetic and copies ran while one was open for 0% of the time, Pallas kernels for 0%

profile of v2, /device:TPU:0, one launch (start us, length us, event | category | flops | bytes accessed | tf_op | source)
XLA Modules:
  0.0 148.2 jit_solution(17495545838618572267)
XLA Ops:
  6.5 0.0 copy-start
  6.5 0.0 all-gather.6.cloned.1.call-start
  6.5 0.8 copy.11
  7.4 0.1 reduce
  7.5 0.1 convert_reduce_fusion
  7.6 0.0 copy-done
  7.6 0.0 copy-start.1
  7.6 0.0 copy-start.2
  7.6 7.2 %fusion.6 = f32[64,2048]{1,0:T(8,128)} fusion(bf16[64,2560]{1,0:T(8,128)(2,1)S(1)} %copy-done, bf16[2560,2048]{1,0:T(8,128)(2,1)} %param.7, s32[2048]{0:T(1024)} %param.9, s32[2560]{0:T(1024)S(1)} %convert_reduce_fusion), kind=kOutput, calls=%fused_computation.9 | convolution fusion | flops 681574400 | bytes 11356160 | tf_op jit(solution)/shard_map/dot_general | solution.py:23
  14.8 0.0 all-gather.6.cloned.1.call-update
  14.8 0.0 all-gather.4.cloned.1.call-start
  14.9 24.1 %all-gather.6.cloned.1.call-done = f32[128,2048]{1,0:T(8,128)} async-done(((f32[64,2048]{1,0:T(8,128)}), f32[128,2048]{1,0:T(8,128)}) %all-gather.6.cloned.1.call-update) | async-done | bytes 1048592 | tf_op jit(solution)/shard_map/all_gather | solution.py:9
  39.0 1.3 reduce_sum.19
  40.3 2.3 %all_gather.14 = bf16[64,4096]{1,0:T(8,128)(2,1)} all-gather(bf16[64,2048]{1,0:T(8,128)(2,1)S(1)} %reduce_sum.19), channel_id=1, replica_groups=mesh['basis'=2,'eig'=8,'chan'=2] {'chan'}, dimensions={1}, use_global_device_ids=true | all-gather | bytes 786432 | tf_op jit(solution)/shard_map/all_gather | solution.py:25
  42.6 0.0 all-gather.4.cloned.1.call-update
  42.6 0.0 copy-done.1
  42.7 0.0 copy-done.2
  42.7 0.1 subtract_divide_fusion
  42.7 72.9 %all-gather.4.cloned.1.call-done = bf16[512,4096]{1,0:T(8,128)(2,1)} async-done(((bf16[64,4096]{1,0:T(8,128)(2,1)}), bf16[512,4096]{1,0:T(8,128)(2,1)}) %all-gather.4.cloned.1.call-update) | async-done | bytes 4194320 | tf_op jit(solution)/shard_map/all_gather | solution.py:32
  115.6 4.1 %dynamic-slice_convert_fusion = f32[512,2048]{1,0:T(8,128)} fusion(bf16[512,4096]{1,0:T(8,128)(2,1)} %all-gather.4.cloned.1.call-done, s32[]{:T(128)S(6)} %select_n.11), kind=kLoop, calls=%fused_computation.10 | loop fusion | flops 1048576 | bytes 6291460 | tf_op jit(solution)/shard_map/convert_element_type | solution.py:35
  119.7 5.3 %copy.12 = f32[512,2048]{0,1:T(8,128)} copy(f32[512,2048]{1,0:T(8,128)} %dynamic-slice_convert_fusion) | data formatting | bytes 8388608 | tf_op jit(solution)/shard_map/convert_element_type | solution.py:35
  125.1 16.3 %convolution_multiply_fusion = f32[8,2048,512]{2,1,0:T(8,128)} fusion(f32[512,2048]{0,1:T(8,128)} %copy.12, f32[8,512]{1,0:T(8,128)S(1)} %subtract_divide_fusion, bf16[512,4096]{1,0:T(8,128)(2,1)} %all-gather.4.cloned.1.call-done, s32[]{:T(128)S(6)} %select_n.12), kind=kOutput, calls=%fused_computation.2 | convolution fusion | flops 8615100416 | bytes 38289412 | tf_op jit(solution)/shard_map/ekc,kd->ecd/dot_general | solution.py:36
  (2 shorter events, 0.0 us)
Async XLA Ops:
  6.5 1.1 copy-start
  6.5 32.4 %all-gather.6.cloned.1.call-start = ((), (), s32[]{:S(2)}) async-start(), calls=%async_computation.1 | async-start | bytes 1572864 | tf_op jit(solution)/shard_map/all_gather | solution.py:9
  7.6 35.1 %copy-start.1 = (f32[512]{0:T(512)S(1)}, f32[512]{0:T(512)}, u32[]{:S(2)}) copy-start(f32[512]{0:T(512)} %param.10) | copy-start | bytes 6148
  7.6 35.0 %copy-start.2 = (f32[8]{0:T(128)S(1)}, f32[8]{0:T(128)}, u32[]{:S(2)}) copy-start(f32[8]{0:T(128)} %param.11) | copy-start | bytes 100
  14.8 100.8 %all-gather.4.cloned.1.call-start = ((), (), s32[]{:S(2)}) async-start(), calls=%async_computation | async-start | bytes 4718592 | tf_op jit(solution)/shard_map/all_gather | solution.py:32
Sparse Core Ops, SparseCore 0:
  14.9 23.9 all-gather.5
  42.8 72.7 all-gather.3
